TPU v7x, 512 devices: a whole 4x4x16 slice. The times are simulated.
512 devices in a mesh: head: 8 (over x, core), expert: 64 (over z, y).
Axes of the slice: x: 4, y: 4, z: 16, core: 2. Of those that a mesh axis runs over, the one named last changes fastest.
Arguments:
- q_latent: bfloat16 [512, 64, 512], P('expert', 'head'), may hold values from -16 to 16
- q_rotary: bfloat16 [512, 64, 64], P('expert', 'head'), may hold values from -3 to 3
- cache_latent: bfloat16 [512, 128, 512], P('expert'), may hold values from -5 to 5
- cache_rotary: bfloat16 [512, 64, 128], P('expert'), may hold values from -5 to 5
- lengths: int32 [512], P('expert'), may hold values from 16 to 128, as said below
- w_value_out: bfloat16 [32768, 5120], P('head', 'expert'), may hold values from -0.25 to 0.25
- resid: bfloat16 [512, 5120], P('expert'), may hold values from -8 to 8
- norm_gain: float32 [5120], replicated, may hold values from 0.1 to 1.9
- route_ids: int32 [512, 6], P('expert'), may hold values from 0 to 63, as said below
- route_weights: float32 [512, 6], P('expert'), may hold values from 0.1 to 0.6
- w_gate_up: bfloat16 [64, 2, 768, 5120], P('expert', None, 'head'), may hold values from -0.078125 to 0.078125
- w_down: bfloat16 [64, 768, 5120], P('expert', 'head'), may hold values from -0.21875 to 0.21875
Outputs:
- mixed_out: float32 [512, 5120], P('expert', 'head')
Inputs may be any that keep to these rules, and one draw needn't show every extreme that they name: `lengths`: slots at positions below a sequence's length are valid; some sequence has length 128. `route_ids`: each row names 6 different experts. Among the rows of one device (aligned blocks of 8 rows) no expert is named by more than 2 rows, and one expert is named by exactly 2 rows in every block.
All inputs are finite; a program needn't handle non-finite values.
Results may differ from a plain program's by a relative error of at most 0.0046.
Values may be sent and summed in bfloat16 or wider, within the bound.
No kernel may reach another device: no remote copies, remote signals or barrier semaphores. Data moves between devices by JAX's collectives and lax.ppermute only.
A program may use at most 64 MiB of HBM per device.

v0:
```python
import jax
import jax.numpy as jnp
from jax import lax
from jax.sharding import Mesh
from jax.sharding import PartitionSpec as P

EXPERT = ("ez", "ey")
softmax_scale = 192.0 ** (-0.5)
norm_epsilon = 1e-06


def attend(q_latent, q_rotary, cache_latent, cache_rotary, lengths):
    scores = jnp.einsum("shl,scl->shc", q_latent, cache_latent, preferred_element_type=jnp.float32)
    scores = scores + jnp.einsum(
        "shr,src->shc", q_rotary, cache_rotary, preferred_element_type=jnp.float32
    )
    scores = scores * softmax_scale
    position = lax.broadcasted_iota(jnp.int32, scores.shape, 2)
    scores = jnp.where(position < lengths[:, None, None], scores, -1e30)
    highest = jnp.max(scores, axis=2, keepdims=True)
    weights = jnp.exp(scores - highest)
    probs = (weights / jnp.sum(weights, axis=2, keepdims=True)).astype(jnp.bfloat16)
    return jnp.einsum(
        "shc,scl->shl", probs, cache_latent, preferred_element_type=jnp.float32
    ).astype(jnp.bfloat16)


def on_device(
    q_latent,
    q_rotary,
    cache_latent,
    cache_rotary,
    lengths,
    w_value_out,
    resid,
    norm_gain,
    route_ids,
    route_weights,
    w_gate_up,
    w_down,
):
    seq_local = q_latent.shape[0]
    latent_out = attend(q_latent, q_rotary, cache_latent, cache_rotary, lengths)
    flattened = latent_out.reshape(seq_local, -1)
    z_count = lax.axis_size("ez")
    latent_copies = jnp.broadcast_to(flattened[None], (z_count,) + flattened.shape)
    gathered = lax.all_to_all(latent_copies, "ez", split_axis=0, concat_axis=0, tiled=True)
    gathered = gathered.reshape(-1, flattened.shape[1])
    value_blocks = lax.all_gather(w_value_out, "ey", axis=0, tiled=False)
    column_terms = jnp.einsum(
        "sk,jkc->sjc", gathered, value_blocks, preferred_element_type=jnp.float32
    ).reshape(gathered.shape[0], -1)
    column_sums = lax.psum(column_terms, "head")
    attention = lax.all_to_all(
        column_sums.astype(jnp.bfloat16), "ez", split_axis=0, concat_axis=1, tiled=True
    )
    stream = resid.astype(jnp.float32) + attention.astype(jnp.float32)
    mean_square = jnp.mean(stream * stream, axis=1, keepdims=True)
    normed = (stream * lax.rsqrt(mean_square + norm_epsilon) * norm_gain).astype(jnp.bfloat16)
    expert_count = lax.axis_size("ez") * lax.axis_size("ey")
    top_count = route_ids.shape[1]
    capacity = max(2, -(-(seq_local * top_count) // expert_count))
    flat_ids = route_ids.reshape(-1)
    one_hot = (flat_ids[:, None] == jnp.arange(expert_count, dtype=jnp.int32)[None, :]).astype(
        jnp.int32
    )
    earlier = jnp.cumsum(one_hot, axis=0) - one_hot
    slot_index = jnp.sum(earlier * one_hot, axis=1)
    target = (flat_ids * capacity + slot_index).reshape(seq_local, top_count)
    places = jnp.arange(expert_count * capacity, dtype=jnp.int32)
    matches = target[None, :, :] == places[:, None, None]
    selector = jnp.sum(matches.astype(jnp.int32), axis=2).astype(jnp.bfloat16)
    blending = jnp.sum(jnp.where(matches, route_weights[None, :, :], 0.0), axis=2)
    gate_up = w_gate_up[0]
    col_width = stream.shape[1] // lax.axis_size("head")
    offset = lax.axis_index("head") * col_width
    normed_cols = lax.dynamic_slice_in_dim(normed, offset, col_width, 1)
    outgoing = jnp.dot(selector, normed_cols, preferred_element_type=jnp.float32).astype(
        jnp.bfloat16
    )
    outgoing = outgoing.reshape(expert_count, capacity, -1)
    arrived = lax.all_to_all(outgoing, EXPERT, split_axis=0, concat_axis=0, tiled=True)
    arrived_cols = arrived.reshape(-1, arrived.shape[2])
    head_count = lax.axis_size("head")
    down_blocks = w_down[0].reshape(w_down.shape[1], head_count, -1)
    arrived_cols, down_blocks = lax.optimization_barrier((arrived_cols, down_blocks))
    down_cols = lax.all_to_all(down_blocks, "head", split_axis=1, concat_axis=0, tiled=True)
    down_cols = down_cols.reshape(-1, down_blocks.shape[2])
    flat_rows = lax.all_gather(arrived_cols, "head", axis=1, tiled=True)
    projected = jnp.einsum("rd,gfd->rgf", flat_rows, gate_up, preferred_element_type=jnp.float32)
    hidden = (jax.nn.silu(projected[:, 0]) * projected[:, 1]).astype(jnp.bfloat16)
    hidden_all = lax.all_gather(hidden, "head", axis=1, tiled=True)
    summed_cols = jnp.dot(hidden_all, down_cols, preferred_element_type=jnp.float32).astype(
        jnp.bfloat16
    )
    summed_rows = summed_cols.reshape(expert_count, capacity, -1)
    returned = lax.all_to_all(summed_rows, EXPERT, split_axis=0, concat_axis=0, tiled=True)
    back_rows = returned.reshape(expert_count * capacity, -1).astype(jnp.float32)
    mixture = jnp.dot(blending.T, back_rows, precision=lax.Precision.HIGHEST)
    stream_cols = lax.dynamic_slice_in_dim(stream, offset, col_width, 1)
    return stream_cols + mixture


def solution(mesh):
    placed = (
        P(EXPERT, "head", None),
        P(EXPERT, "head", None),
        P(EXPERT, None, None),
        P(EXPERT, None, None),
        P(EXPERT),
        P("head", EXPERT),
        P(EXPERT, None),
        P(),
        P(EXPERT, None),
        P(EXPERT, None),
        P(EXPERT, None, "head", None),
        P(EXPERT, "head", None),
    )
    head_count, expert_total = mesh.devices.shape
    y_count = len({device.coords[1] for device in mesh.devices[0]})
    split_mesh = Mesh(
        mesh.devices.reshape(head_count, expert_total // y_count, y_count), ("head",) + EXPERT
    )
    return jax.shard_map(
        on_device, mesh=split_mesh, in_specs=placed, out_specs=P(EXPERT, "head"), check_vma=False
    )
```

profile of v0, /device:TPU:8, one launch (start us, length us, event | category | flops | bytes accessed | tf_op | source)
XLA Modules:
  0.0 234.2 jit_solution(10736050746131402408)
XLA Ops:
  7.3 1.6 fusion.20
  8.9 1.1 fusion.8
  10.5 1.1 broadcast_in_dim.33
  11.6 15.2 %all-to-all-start = ((bf16[16,8,4096]{2,1,0:T(8,128)(2,1)}), bf16[16,8,4096]{2,1,0:T(8,128)(2,1)S(1)}, u32[]{:S(2)}, u32[]{:S(2)}) async-start(bf16[16,8,4096]{2,1,0:T(8,128)(2,1)} %broadcast_in_dim.33), calls=%async_computation | async-start | bytes 2097152 | tf_op jit(solution)/shard_map/all_to_all | solution.py:47
  27.3 28.6 %all-gather.6.cloned.1.call-done = bf16[16384,80]{0,1:T(8,128)(2,1)} async-done(((bf16[4096,80]{0,1:T(8,128)(2,1)}), bf16[16384,80]{0,1:T(8,128)(2,1)}) %all-gather.6.cloned.1.call-update) | async-done | bytes 2621456 | tf_op jit(solution)/shard_map/all_gather | solution.py:49
  55.9 5.5 %reshape.55 = bf16[4,4096,80]{1,0,2:T(4,128)(2,1)} reshape(bf16[16384,80]{0,1:T(8,128)(2,1)} %all-gather.6.cloned.1.call-done) | data formatting | bytes 5242880 | tf_op jit(solution)/shard_map/all_gather | solution.py:49
  61.4 4.7 %copy.24 = bf16[4,80,4096]{2,1,0:T(8,128)(2,1)} copy(bf16[4,80,4096]{2,0,1:T(4,128)(2,1)} %bitcast.50) | data formatting | bytes 5242880 | tf_op jit(solution)/shard_map/sk,jkc->sjc/dot_general | solution.py:50
  66.1 10.7 %all-to-all-done = bf16[16,8,4096]{2,1,0:T(8,128)(2,1)S(1)} async-done(((bf16[16,8,4096]{2,1,0:T(8,128)(2,1)}), bf16[16,8,4096]{2,1,0:T(8,128)(2,1)S(1)}, u32[]{:S(2)}, u32[]{:S(2)}) %all-to-all-start) | async-done | bytes 1048608 | tf_op jit(solution)/shard_map/all_to_all | solution.py:47
  76.8 2.6 %fusion.9 = f32[128,320]{0,1:T(8,128)S(1)} fusion(bf16[320,4096]{1,0:T(8,128)(2,1)} %bitcast.49, bf16[16,8,4096]{2,1,0:T(8,128)(2,1)S(1)} %all-to-all-done), kind=kOutput, calls=%fused_computation.14 | convolution fusion | flops 335544320 | bytes 3833856 | tf_op jit(solution)/shard_map/sk,jkc->sjc/dot_general | solution.py:50
  79.4 25.1 %all-reduce.1 = bf16[128,320]{0,1:T(8,128)(2,1)S(1)} all-reduce(f32[128,320]{0,1:T(8,128)S(1)} %fusion.9), channel_id=1, replica_groups=mesh['head'=8,'ez'=16,'ey'=4] {'head'}, use_global_device_ids=true, to_apply=%region_2.3 | all-reduce | flops 40960 | bytes 245760 | tf_op jit(solution)/shard_map/psum | solution.py:53
  105.2 10.2 %all-to-all-start.1 = ((bf16[16,8,320]{2,1,0:T(8,128)(2,1)}), bf16[16,8,320]{2,1,0:T(8,128)(2,1)S(1)}, u32[]{:S(2)}, u32[]{:S(2)}) async-start(bf16[16,8,320]{2,1,0:T(8,128)(2,1)} %bitcast.3), calls=%async_computation.1 | async-start | bytes 196608 | tf_op jit(solution)/shard_map/all_to_all | solution.py:54
  115.6 0.8 dynamic-slice
  116.4 12.1 %all-to-all-done.1 = bf16[16,8,320]{2,1,0:T(8,128)(2,1)S(1)} async-done(((bf16[16,8,320]{2,1,0:T(8,128)(2,1)}), bf16[16,8,320]{2,1,0:T(8,128)(2,1)S(1)}, u32[]{:S(2)}, u32[]{:S(2)}) %all-to-all-start.1) | async-done | bytes 81952 | tf_op jit(solution)/shard_map/all_to_all | solution.py:54
  129.9 7.0 %all-to-all-start.2 = ((bf16[64,2,640]{2,1,0:T(2,128)(2,1)}), bf16[64,2,640]{2,1,0:T(2,128)(2,1)S(1)}, u32[]{:S(2)}, u32[]{:S(2)}) async-start(bf16[64,2,640]{2,1,0:T(2,128)(2,1)} %reshape.49), calls=%async_computation.2 | async-start | bytes 327680 | tf_op jit(solution)/shard_map/all_to_all | solution.py:82
  136.9 1.3 copy.31
  138.2 14.4 %all-to-all-done.2 = bf16[64,2,640]{2,1,0:T(2,128)(2,1)S(1)} async-done(((bf16[64,2,640]{2,1,0:T(2,128)(2,1)}), bf16[64,2,640]{2,1,0:T(2,128)(2,1)S(1)}, u32[]{:S(2)}, u32[]{:S(2)}) %all-to-all-start.2) | async-done | bytes 163872 | tf_op jit(solution)/shard_map/all_to_all | solution.py:82
  153.3 1.1 copy.29
  154.4 5.0 %all-to-all-start.3 = ((bf16[96,8,640]{2,0,1:T(8,128)(2,1)}), bf16[96,8,640]{2,0,1:T(8,128)(2,1)S(1)}, u32[]{:S(2)}, u32[]{:S(2)}) async-start(bf16[96,8,640]{2,0,1:T(8,128)(2,1)} %copy.29), calls=%async_computation.3 | async-start | bytes 1966080 | tf_op jit(solution)/shard_map/all_to_all | solution.py:87
  159.4 19.3 %all-gather.4.cloned.1.call-done = bf16[128,5120]{1,0:T(8,128)(2,1)} async-done(((bf16[128,640]{1,0:T(8,128)(2,1)}), bf16[128,5120]{1,0:T(8,128)(2,1)}) %all-gather.4.cloned.1.call-update) | async-done | bytes 1310736 | tf_op jit(solution)/shard_map/all_gather | solution.py:89
  178.7 2.0 fusion.1
  180.8 12.8 %all_gather.15 = bf16[128,768]{0,1:T(8,128)(2,1)S(1)} all-gather(bf16[128,96]{0,1:T(8,128)(2,1)S(1)} %fusion.12), channel_id=1, replica_groups=mesh['head'=8,'ez'=16,'ey'=4] {'head'}, dimensions={1}, use_global_device_ids=true | all-gather | bytes 221184 | tf_op jit(solution)/shard_map/all_gather | solution.py:92
  194.6 13.5 %all-to-all-start.4 = ((bf16[64,2,640]{2,1,0:T(2,128)(2,1)}), bf16[64,2,640]{2,1,0:T(2,128)(2,1)S(1)}, u32[]{:S(2)}, u32[]{:S(2)}) async-start(bf16[64,2,640]{2,1,0:T(2,128)(2,1)} %reshape.52), calls=%async_computation.4 | async-start | bytes 327680 | tf_op jit(solution)/shard_map/all_to_all | solution.py:97
  208.3 18.2 %all-to-all-done.4 = bf16[64,2,640]{2,1,0:T(2,128)(2,1)S(1)} async-done(((bf16[64,2,640]{2,1,0:T(2,128)(2,1)}), bf16[64,2,640]{2,1,0:T(2,128)(2,1)S(1)}, u32[]{:S(2)}, u32[]{:S(2)}) %all-to-all-start.4) | async-done | bytes 163872 | tf_op jit(solution)/shard_map/all_to_all | solution.py:97
  226.6 0.8 convolution_add_fusion.1
  (41 shorter events, 6.1 us)
Async XLA Ops:
  6.5 172.2 %copy-start = (bf16[1,2,96,5120]{3,2,1,0:T(8,128)(2,1)S(1)}, bf16[1,2,96,5120]{3,2,1,0:T(8,128)(2,1)}, u32[]{:S(2)}) copy-start(bf16[1,2,96,5120]{3,2,1,0:T(8,128)(2,1)} %param.22) | copy-start | bytes 5898244
  6.5 3.6 %copy-start.1 = (bf16[8,128,512]{2,1,0:T(8,128)(2,1)S(1)}, bf16[8,128,512]{2,1,0:T(8,128)(2,1)}, u32[]{:S(2)}) copy-start(bf16[8,128,512]{2,1,0:T(8,128)(2,1)} %param.14) | copy-start | bytes 3145732
  6.5 49.3 %all-gather.6.cloned.1.call-start = ((), (), s32[]{:S(2)}) async-start(), calls=%async_computation.6 | async-start | bytes 3276800 | tf_op jit(solution)/shard_map/all_gather | solution.py:49
  10.4 16.4 %copy-start.3 = (s32[8,6]{1,0:T(8,128)S(1)}, s32[8,6]{1,0:T(8,128)}, u32[]{:S(2)}) copy-start(s32[8,6]{1,0:T(8,128)} %param.20) | copy-start | bytes 580
  11.6 65.2 %all-to-all-start = ((bf16[16,8,4096]{2,1,0:T(8,128)(2,1)}), bf16[16,8,4096]{2,1,0:T(8,128)(2,1)S(1)}, u32[]{:S(2)}, u32[]{:S(2)}) async-start(bf16[16,8,4096]{2,1,0:T(8,128)(2,1)} %broadcast_in_dim.33), calls=%async_computation | async-start | bytes 2097152 | tf_op jit(solution)/shard_map/all_to_all | solution.py:47
  76.8 51.9 %copy-start.2 = (bf16[8,5120]{1,0:T(8,128)(2,1)S(1)}, bf16[8,5120]{1,0:T(8,128)(2,1)}, u32[]{:S(2)}) copy-start(bf16[8,5120]{1,0:T(8,128)(2,1)} %param.18) | copy-start | bytes 245764
  105.2 23.2 %all-to-all-start.1 = ((bf16[16,8,320]{2,1,0:T(8,128)(2,1)}), bf16[16,8,320]{2,1,0:T(8,128)(2,1)S(1)}, u32[]{:S(2)}, u32[]{:S(2)}) async-start(bf16[16,8,320]{2,1,0:T(8,128)(2,1)} %bitcast.3), calls=%async_computation.1 | async-start | bytes 196608 | tf_op jit(solution)/shard_map/all_to_all | solution.py:54
  129.9 22.7 %all-to-all-start.2 = ((bf16[64,2,640]{2,1,0:T(2,128)(2,1)}), bf16[64,2,640]{2,1,0:T(2,128)(2,1)S(1)}, u32[]{:S(2)}, u32[]{:S(2)}) async-start(bf16[64,2,640]{2,1,0:T(2,128)(2,1)} %reshape.49), calls=%async_computation.2 | async-start | bytes 327680 | tf_op jit(solution)/shard_map/all_to_all | solution.py:82
  136.8 41.9 %all-gather.4.cloned.1.call-start = ((), (), s32[]{:S(2)}) async-start(), calls=%async_computation.5 | async-start | bytes 1474560 | tf_op jit(solution)/shard_map/all_gather | solution.py:89
  154.4 39.1 %all-to-all-start.3 = ((bf16[96,8,640]{2,0,1:T(8,128)(2,1)}), bf16[96,8,640]{2,0,1:T(8,128)(2,1)S(1)}, u32[]{:S(2)}, u32[]{:S(2)}) async-start(bf16[96,8,640]{2,0,1:T(8,128)(2,1)} %copy.29), calls=%async_computation.3 | async-start | bytes 1966080 | tf_op jit(solution)/shard_map/all_to_all | solution.py:87
  180.7 27.4 %copy-start.4 = (f32[8,6]{1,0:T(8,128)S(1)}, f32[8,6]{1,0:T(8,128)}, u32[]{:S(2)}) copy-start(f32[8,6]{1,0:T(8,128)} %param.21) | copy-start | bytes 580
  194.6 31.9 %all-to-all-start.4 = ((bf16[64,2,640]{2,1,0:T(2,128)(2,1)}), bf16[64,2,640]{2,1,0:T(2,128)(2,1)S(1)}, u32[]{:S(2)}, u32[]{:S(2)}) async-start(bf16[64,2,640]{2,1,0:T(2,128)(2,1)} %reshape.52), calls=%async_computation.4 | async-start | bytes 327680 | tf_op jit(solution)/shard_map/all_to_all | solution.py:97
Sparse Core Ops, SparseCore 0:
  9.5 46.3 all-gather.5
  153.5 25.2 all-gather.3
where the time goes:
time: 235 us; the launch traced here: 234 us
  waiting for transfers between devices  104 us (44%)
  starting transfers between devices  50.9 us (22%)
  blocking collectives  37.9 us (16%)
  local copies, waits for them, and re-layouts  18 us (8%)
  between operations  13.6 us (6%)
  matrix products  9.05 us (4%)
    all_gather x1, waiting for transfers between devices, on_device(): value_blocks = lax.all_gather(w_value_out, 'ey', axis=0, tiled=False)  28.6 us
    psum x1, blocking collectives, on_device(): column_sums = lax.psum(column_terms, 'head')  25.1 us
    all_gather x1, waiting for transfers between devices, on_device(): flat_rows = lax.all_gather(arrived_cols, 'head', axis=1, tiled=True)  19.3 us
    all_to_all x1, waiting for transfers between devices, on_device(): lax.all_to_all(summed_rows, EXPERT, split_axis=0, concat_axis=0, tiled=True)  18.2 us
    all_to_all x1, starting transfers between devices, on_device(): lax.all_to_all(latent_copies, 'ez', split_axis=0, concat_axis=0, tiled=True)  15.2 us
    all_to_all x1, waiting for transfers between devices, on_device(): lax.all_to_all(outgoing, EXPERT, split_axis=0, concat_axis=0, tiled=True)  14.4 us
    all_to_all x1, starting transfers between devices, on_device(): lax.all_to_all(summed_rows, EXPERT, split_axis=0, concat_axis=0, tiled=True)  13.5 us
    all_gather x1, blocking collectives, on_device(): hidden_all = lax.all_gather(hidden, 'head', axis=1, tiled=True)  12.8 us
  transfers between devices with their start and end apart: 7, of which 6 were waited for; matrix products, arithmetic and copies ran while one was open for 9% of the time, Pallas kernels for 0%

commit v1 on v0

--- a/solution.py
+++ b/solution.py
@@ -7,6 +7,19 @@
 EXPERT = ("ez", "ey")
 softmax_scale = 192.0 ** (-0.5)
 norm_epsilon = 1e-06
+
+
+def ring_gather(value, axis, dim):
+    ways = lax.axis_size(axis)
+    up = [(d, (d + 1) % ways) for d in range(ways)]
+    down = [(d, (d - 1) % ways) for d in range(ways)]
+    earlier, later = ([value], [value])
+    for _ in range(ways // 2):
+        earlier.append(lax.ppermute(earlier[-1], axis, up))
+    for _ in range((ways - 1) // 2):
+        later.append(lax.ppermute(later[-1], axis, down))
+    line = jnp.concatenate([*earlier[::-1], *later[1:]], axis=dim)
+    return jnp.roll(line, (lax.axis_index(axis) - ways // 2) * value.shape[dim], axis=dim)
 
 
 def attend(q_latent, q_rotary, cache_latent, cache_rotary, lengths):
@@ -86,7 +99,7 @@
     arrived_cols, down_blocks = lax.optimization_barrier((arrived_cols, down_blocks))
     down_cols = lax.all_to_all(down_blocks, "head", split_axis=1, concat_axis=0, tiled=True)
     down_cols = down_cols.reshape(-1, down_blocks.shape[2])
-    flat_rows = lax.all_gather(arrived_cols, "head", axis=1, tiled=True)
+    flat_rows = ring_gather(arrived_cols, "head", 1)
     projected = jnp.einsum("rd,gfd->rgf", flat_rows, gate_up, preferred_element_type=jnp.float32)
     hidden = (jax.nn.silu(projected[:, 0]) * projected[:, 1]).astype(jnp.bfloat16)
     hidden_all = lax.all_gather(hidden, "head", axis=1, tiled=True)

time: 235 us -> 244 us (1.038)
  the two profiles are of different devices: /device:TPU:8 before, /device:TPU:2 now
where the time goes in v1:
time: 244 us; the launch traced here: 243 us
  waiting for transfers between devices  107 us (44%)
  starting transfers between devices  52.1 us (21%)
  blocking collectives  34.8 us (14%)
  local copies, waits for them, and re-layouts  24.8 us (10%)
  between operations  13.7 us (6%)
  matrix products  9.82 us (4%)
    all_gather x1, waiting for transfers between devices, on_device(): value_blocks = lax.all_gather(w_value_out, 'ey', axis=0, tiled=False)  28.3 us
    psum x1, blocking collectives, on_device(): column_sums = lax.psum(column_terms, 'head')  22 us
    all_to_all x1, waiting for transfers between devices, on_device(): lax.all_to_all(summed_rows, EXPERT, split_axis=0, concat_axis=0, tiled=True)  19.6 us
    all_to_all x1, waiting for transfers between devices, on_device(): lax.all_to_all(outgoing, EXPERT, split_axis=0, concat_axis=0, tiled=True)  15.4 us
    all_to_all x1, starting transfers between devices, on_device(): lax.all_to_all(latent_copies, 'ez', split_axis=0, concat_axis=0, tiled=True)  15.2 us
    all_gather x1, blocking collectives, on_device(): hidden_all = lax.all_gather(hidden, 'head', axis=1, tiled=True)  12.8 us
    all_to_all x1, waiting for transfers between devices, on_device(): lax.all_to_all(column_sums.astype(jnp.bfloat16), 'ez', split_axis=0, conc...  12.1 us
    all_to_all x1, starting transfers between devices, on_device(): lax.all_to_all(down_blocks, 'head', split_axis=1, concat_axis=0, tiled=True)  11 us
  transfers between devices with their start and end apart: 13, of which 9 were waited for; matrix products, arithmetic and copies ran while one was open for 11% of the time, Pallas kernels for 0%

profile of v1, /device:TPU:2, one launch (start us, length us, event | category | flops | bytes accessed | tf_op | source)
XLA Modules:
  0.0 243.2 jit_solution(5605383662681984592)
XLA Ops:
  7.3 1.6 fusion.22
  10.1 1.5 fusion.5
  12.8 15.2 %all-to-all-start = ((bf16[16,8,4096]{2,1,0:T(8,128)(2,1)}), bf16[16,8,4096]{2,1,0:T(8,128)(2,1)S(1)}, u32[]{:S(2)}, u32[]{:S(2)}) async-start(bf16[16,8,4096]{2,1,0:T(8,128)(2,1)} %broadcast_in_dim.33), calls=%async_computation | async-start | bytes 2097152 | tf_op jit(solution)/shard_map/all_to_all | solution.py:60
  28.5 28.3 %all-gather.3.cloned.1.call-done = bf16[16384,80]{0,1:T(8,128)(2,1)} async-done(((bf16[4096,80]{0,1:T(8,128)(2,1)}), bf16[16384,80]{0,1:T(8,128)(2,1)}) %all-gather.3.cloned.1.call-update) | async-done | bytes 2621456 | tf_op jit(solution)/shard_map/all_gather | solution.py:62
  56.8 5.5 %reshape.55 = bf16[4,4096,80]{1,0,2:T(4,128)(2,1)} reshape(bf16[16384,80]{0,1:T(8,128)(2,1)} %all-gather.3.cloned.1.call-done) | data formatting | bytes 5242880 | tf_op jit(solution)/shard_map/all_gather | solution.py:62
  62.4 4.7 %copy.24 = bf16[4,80,4096]{2,1,0:T(8,128)(2,1)} copy(bf16[4,80,4096]{2,0,1:T(4,128)(2,1)} %bitcast.50) | data formatting | bytes 5242880 | tf_op jit(solution)/shard_map/sk,jkc->sjc/dot_general | solution.py:63
  67.0 11.0 %all-to-all-done = bf16[16,8,4096]{2,1,0:T(8,128)(2,1)S(1)} async-done(((bf16[16,8,4096]{2,1,0:T(8,128)(2,1)}), bf16[16,8,4096]{2,1,0:T(8,128)(2,1)S(1)}, u32[]{:S(2)}, u32[]{:S(2)}) %all-to-all-start) | async-done | bytes 1048608 | tf_op jit(solution)/shard_map/all_to_all | solution.py:60
  78.0 2.6 %fusion.10 = f32[128,320]{0,1:T(8,128)S(1)} fusion(bf16[320,4096]{1,0:T(8,128)(2,1)} %bitcast.49, bf16[16,8,4096]{2,1,0:T(8,128)(2,1)S(1)} %all-to-all-done), kind=kOutput, calls=%fused_computation.15 | convolution fusion | flops 335544320 | bytes 3833856 | tf_op jit(solution)/shard_map/sk,jkc->sjc/dot_general | solution.py:63
  80.6 22.0 %all-reduce.1 = bf16[128,320]{0,1:T(8,128)(2,1)S(1)} all-reduce(f32[128,320]{0,1:T(8,128)S(1)} %fusion.10), channel_id=1, replica_groups=mesh['head'=8,'ez'=16,'ey'=4] {'head'}, use_global_device_ids=true, to_apply=%region_2.3 | all-reduce | flops 40960 | bytes 245760 | tf_op jit(solution)/shard_map/psum | solution.py:66
  103.4 10.2 %all-to-all-start.1 = ((bf16[16,8,320]{2,1,0:T(8,128)(2,1)}), bf16[16,8,320]{2,1,0:T(8,128)(2,1)S(1)}, u32[]{:S(2)}, u32[]{:S(2)}) async-start(bf16[16,8,320]{2,1,0:T(8,128)(2,1)} %bitcast.3), calls=%async_computation.1 | async-start | bytes 196608 | tf_op jit(solution)/shard_map/all_to_all | solution.py:67
  114.6 12.1 %all-to-all-done.1 = bf16[16,8,320]{2,1,0:T(8,128)(2,1)S(1)} async-done(((bf16[16,8,320]{2,1,0:T(8,128)(2,1)}), bf16[16,8,320]{2,1,0:T(8,128)(2,1)S(1)}, u32[]{:S(2)}, u32[]{:S(2)}) %all-to-all-start.1) | async-done | bytes 81952 | tf_op jit(solution)/shard_map/all_to_all | solution.py:67
  128.6 7.0 %all-to-all-start.2 = ((bf16[64,2,640]{2,1,0:T(2,128)(2,1)}), bf16[64,2,640]{2,1,0:T(2,128)(2,1)S(1)}, u32[]{:S(2)}, u32[]{:S(2)}) async-start(bf16[64,2,640]{2,1,0:T(2,128)(2,1)} %reshape.49), calls=%async_computation.2 | async-start | bytes 327680 | tf_op jit(solution)/shard_map/all_to_all | solution.py:95
  135.6 1.3 copy.31
  137.0 15.4 %all-to-all-done.2 = bf16[64,2,640]{2,1,0:T(2,128)(2,1)S(1)} async-done(((bf16[64,2,640]{2,1,0:T(2,128)(2,1)}), bf16[64,2,640]{2,1,0:T(2,128)(2,1)S(1)}, u32[]{:S(2)}, u32[]{:S(2)}) %all-to-all-start.2) | async-done | bytes 163872 | tf_op jit(solution)/shard_map/all_to_all | solution.py:95
  152.5 4.7 %collective-permute-done = bf16[128,640]{1,0:T(8,128)(2,1)S(1)} collective-permute-done((bf16[128,640]{1,0:T(8,128)(2,1)S(1)}, bf16[128,640]{1,0:T(8,128)(2,1)S(1)}, u32[]{:S(2)}, u32[]{:S(2)}) %collective-permute-start) | collective-permute-done | bytes 163872 | tf_op jit(solution)/shard_map/ppermute | solution.py:18
  157.8 1.1 collective-permute-start.4
  159.0 3.0 %collective-permute-done.1 = bf16[128,640]{1,0:T(8,128)(2,1)S(1)} collective-permute-done((bf16[128,640]{1,0:T(8,128)(2,1)S(1)}, bf16[128,640]{1,0:T(8,128)(2,1)S(1)}, u32[]{:S(2)}, u32[]{:S(2)}) %collective-permute-start.1) | collective-permute-done | bytes 163872 | tf_op jit(solution)/shard_map/ppermute | solution.py:18
  163.8 3.1 %collective-permute-done.2 = bf16[128,640]{1,0:T(8,128)(2,1)} collective-permute-done((bf16[128,640]{1,0:T(8,128)(2,1)S(1)}, bf16[128,640]{1,0:T(8,128)(2,1)}, u32[]{:S(2)}, u32[]{:S(2)}) %collective-permute-start.2) | collective-permute-done | bytes 163872 | tf_op jit(solution)/shard_map/ppermute | solution.py:18
  168.4 11.0 %all-to-all-start.3 = ((bf16[96,8,640]{2,0,1:T(8,128)(2,1)}), bf16[96,8,640]{2,0,1:T(8,128)(2,1)S(1)}, u32[]{:S(2)}, u32[]{:S(2)}) async-start(bf16[96,8,640]{2,0,1:T(8,128)(2,1)} %copy.29), calls=%async_computation.3 | async-start | bytes 1966080 | tf_op jit(solution)/shard_map/all_to_all | solution.py:100
  183.4 9.2 %collective-permute-done.6 = bf16[128,640]{1,0:T(8,128)(2,1)S(1)} collective-permute-done((bf16[128,640]{1,0:T(8,128)(2,1)}, bf16[128,640]{1,0:T(8,128)(2,1)S(1)}, u32[]{:S(2)}, u32[]{:S(2)}) %collective-permute-start.6) | collective-permute-done | bytes 163872 | tf_op jit(solution)/shard_map/ppermute | solution.py:20
  196.5 12.8 %all_gather.11 = bf16[128,768]{0,1:T(8,128)(2,1)S(1)} all-gather(bf16[128,96]{0,1:T(8,128)(2,1)S(1)} %fusion.13), channel_id=1, replica_groups=mesh['head'=8,'ez'=16,'ey'=4] {'head'}, dimensions={1}, use_global_device_ids=true | all-gather | bytes 221184 | tf_op jit(solution)/shard_map/all_gather | solution.py:105
  210.3 4.6 %all-to-all-start.4 = ((bf16[64,2,640]{2,1,0:T(2,128)(2,1)}), bf16[64,2,640]{2,1,0:T(2,128)(2,1)S(1)}, u32[]{:S(2)}, u32[]{:S(2)}) async-start(bf16[64,2,640]{2,1,0:T(2,128)(2,1)} %reshape.52), calls=%async_computation.4 | async-start | bytes 327680 | tf_op jit(solution)/shard_map/all_to_all | solution.py:110
  215.1 19.6 %all-to-all-done.4 = bf16[64,2,640]{2,1,0:T(2,128)(2,1)S(1)} async-done(((bf16[64,2,640]{2,1,0:T(2,128)(2,1)}), bf16[64,2,640]{2,1,0:T(2,128)(2,1)S(1)}, u32[]{:S(2)}, u32[]{:S(2)}) %all-to-all-start.4) | async-done | bytes 163872 | tf_op jit(solution)/shard_map/all_to_all | solution.py:110
  234.8 1.5 convolution_add_fusion.1
  (72 shorter events, 20.3 us)
Async XLA Ops:
  6.5 189.1 %copy-start = (bf16[1,2,96,5120]{3,2,1,0:T(8,128)(2,1)S(1)}, bf16[1,2,96,5120]{3,2,1,0:T(8,128)(2,1)}, u32[]{:S(2)}) copy-start(bf16[1,2,96,5120]{3,2,1,0:T(8,128)(2,1)} %param.22) | copy-start | bytes 5898244
  6.5 50.3 %all-gather.3.cloned.1.call-start = ((), (), s32[]{:S(2)}) async-start(), calls=%async_computation.5 | async-start | bytes 3276800 | tf_op jit(solution)/shard_map/all_gather | solution.py:62
  8.9 19.2 %copy-start.5 = (s32[8,6]{1,0:T(8,128)S(1)}, s32[8,6]{1,0:T(8,128)}, u32[]{:S(2)}) copy-start(s32[8,6]{1,0:T(8,128)} %param.20) | copy-start | bytes 580
  12.8 65.2 %all-to-all-start = ((bf16[16,8,4096]{2,1,0:T(8,128)(2,1)}), bf16[16,8,4096]{2,1,0:T(8,128)(2,1)S(1)}, u32[]{:S(2)}, u32[]{:S(2)}) async-start(bf16[16,8,4096]{2,1,0:T(8,128)(2,1)} %broadcast_in_dim.33), calls=%async_computation | async-start | bytes 2097152 | tf_op jit(solution)/shard_map/all_to_all | solution.py:60
  78.0 48.8 %copy-start.4 = (bf16[8,5120]{1,0:T(8,128)(2,1)S(1)}, bf16[8,5120]{1,0:T(8,128)(2,1)}, u32[]{:S(2)}) copy-start(bf16[8,5120]{1,0:T(8,128)(2,1)} %param.18) | copy-start | bytes 245764
  103.4 23.2 %all-to-all-start.1 = ((bf16[16,8,320]{2,1,0:T(8,128)(2,1)}), bf16[16,8,320]{2,1,0:T(8,128)(2,1)S(1)}, u32[]{:S(2)}, u32[]{:S(2)}) async-start(bf16[16,8,320]{2,1,0:T(8,128)(2,1)} %bitcast.3), calls=%async_computation.1 | async-start | bytes 196608 | tf_op jit(solution)/shard_map/all_to_all | solution.py:67
  127.0 0.7 copy-start.3
  128.6 23.8 %all-to-all-start.2 = ((bf16[64,2,640]{2,1,0:T(2,128)(2,1)}), bf16[64,2,640]{2,1,0:T(2,128)(2,1)S(1)}, u32[]{:S(2)}, u32[]{:S(2)}) async-start(bf16[64,2,640]{2,1,0:T(2,128)(2,1)} %reshape.49), calls=%async_computation.2 | async-start | bytes 327680 | tf_op jit(solution)/shard_map/all_to_all | solution.py:95
  152.5 4.8 %collective-permute-start = (bf16[128,640]{1,0:T(8,128)(2,1)S(1)}, bf16[128,640]{1,0:T(8,128)(2,1)S(1)}, u32[]{:S(2)}, u32[]{:S(2)}) collective-permute-start(bf16[128,640]{1,0:T(8,128)(2,1)S(1)} %reshape.50), channel_id=1, source_target_pairs={{0,64},{64,128},{128,192},{192,256},{256,320},{320,384},{384,448},... | collective-permute-start | bytes 491528 | tf_op jit(solution)/shard_map/ppermute | solution.py:18
  157.2 4.7 %collective-permute-start.1 = (bf16[128,640]{1,0:T(8,128)(2,1)S(1)}, bf16[128,640]{1,0:T(8,128)(2,1)S(1)}, u32[]{:S(2)}, u32[]{:S(2)}) collective-permute-start(bf16[128,640]{1,0:T(8,128)(2,1)S(1)} %collective-permute-done), channel_id=1, source_target_pairs={{0,64},{64,128},{128,192},{192,256},{256,320},{320,384},{384,448},... | collective-permute-start | bytes 491528 | tf_op jit(solution)/shard_map/ppermute | solution.py:18
  157.8 4.7 %collective-permute-start.4 = (bf16[128,640]{1,0:T(8,128)(2,1)S(1)}, bf16[128,640]{1,0:T(8,128)(2,1)S(1)}, u32[]{:S(2)}, u32[]{:S(2)}) collective-permute-start(bf16[128,640]{1,0:T(8,128)(2,1)S(1)} %reshape.50), channel_id=1, source_target_pairs={{0,448},{64,0},{128,64},{192,128},{256,192},{320,256},{384,320},{4... | collective-permute-start | bytes 491528 | tf_op jit(solution)/shard_map/ppermute | solution.py:20
  162.0 0.7 copy-start.1
  162.0 4.8 %collective-permute-start.2 = (bf16[128,640]{1,0:T(8,128)(2,1)S(1)}, bf16[128,640]{1,0:T(8,128)(2,1)}, u32[]{:S(2)}, u32[]{:S(2)}) collective-permute-start(bf16[128,640]{1,0:T(8,128)(2,1)S(1)} %collective-permute-done.1), channel_id=1, source_target_pairs={{0,64},{64,128},{128,192},{192,256},{256,320},{320,384},{384,448},... | collective-permute-start | bytes 491528 | tf_op jit(solution)/shard_map/ppermute | solution.py:18
  162.7 16.7 %collective-permute-start.5 = (bf16[128,640]{1,0:T(8,128)(2,1)S(1)}, bf16[128,640]{1,0:T(8,128)(2,1)}, u32[]{:S(2)}, u32[]{:S(2)}) collective-permute-start(bf16[128,640]{1,0:T(8,128)(2,1)S(1)} %collective-permute-done.4), channel_id=1, source_target_pairs={{0,448},{64,0},{128,64},{192,128},{256,192},{320,256},{384,320},{4... | collective-permute-start | bytes 491528 | tf_op jit(solution)/shard_map/ppermute | solution.py:20
  166.8 12.7 %collective-permute-start.3 = (bf16[128,640]{1,0:T(8,128)(2,1)}, bf16[128,640]{1,0:T(8,128)(2,1)}, u32[]{:S(2)}, u32[]{:S(2)}) collective-permute-start(bf16[128,640]{1,0:T(8,128)(2,1)} %collective-permute-done.2), channel_id=1, source_target_pairs={{0,64},{64,128},{128,192},{192,256},{256,320},{320,384},{384,448},... | collective-permute-start | bytes 491528 | tf_op jit(solution)/shard_map/ppermute | solution.py:18
  168.4 40.9 %all-to-all-start.3 = ((bf16[96,8,640]{2,0,1:T(8,128)(2,1)}), bf16[96,8,640]{2,0,1:T(8,128)(2,1)S(1)}, u32[]{:S(2)}, u32[]{:S(2)}) async-start(bf16[96,8,640]{2,0,1:T(8,128)(2,1)} %copy.29), calls=%async_computation.3 | async-start | bytes 1966080 | tf_op jit(solution)/shard_map/all_to_all | solution.py:100
  179.4 15.1 %copy-start.2 = (bf16[128,640]{1,0:T(8,128)(2,1)S(1)}, bf16[128,640]{1,0:T(8,128)(2,1)}, u32[]{:S(2)}) copy-start(bf16[128,640]{1,0:T(8,128)(2,1)} %copy-done.1) | copy-start | bytes 491524
  179.4 13.2 %collective-permute-start.6 = (bf16[128,640]{1,0:T(8,128)(2,1)}, bf16[128,640]{1,0:T(8,128)(2,1)S(1)}, u32[]{:S(2)}, u32[]{:S(2)}) collective-permute-start(bf16[128,640]{1,0:T(8,128)(2,1)} %collective-permute-done.5), channel_id=1, source_target_pairs={{0,448},{64,0},{128,64},{192,128},{256,192},{320,256},{384,320},{4... | collective-permute-start | bytes 491528 | tf_op jit(solution)/shard_map/ppermute | solution.py:20
  195.6 19.3 %copy-start.6 = (f32[8,6]{1,0:T(8,128)S(1)}, f32[8,6]{1,0:T(8,128)}, u32[]{:S(2)}) copy-start(f32[8,6]{1,0:T(8,128)} %param.21) | copy-start | bytes 580
  210.3 24.4 %all-to-all-start.4 = ((bf16[64,2,640]{2,1,0:T(2,128)(2,1)}), bf16[64,2,640]{2,1,0:T(2,128)(2,1)S(1)}, u32[]{:S(2)}, u32[]{:S(2)}) async-start(bf16[64,2,640]{2,1,0:T(2,128)(2,1)} %reshape.52), calls=%async_computation.4 | async-start | bytes 327680 | tf_op jit(solution)/shard_map/all_to_all | solution.py:110
Sparse Core Ops, SparseCore 0:
  9.5 47.3 all-gather.2
